TPU v7x, 256 devices: a whole 4x4x8 slice. The times are simulated.
256 devices in a mesh: corpus: 32 (over z, x), group: 8 (over y, core).
Axes of the slice: x: 4, y: 4, z: 8, core: 2. Of those that a mesh axis runs over, the one named last changes fastest.
Arguments:
- embeddings: float32 [196608, 768], P(('corpus', 'group')), may hold values from -150 to 150
- labels: int32 [196608, 1], P(('corpus', 'group')), may hold values from 0 to 255, as said below
- neighbours: int32 [256], replicated, may hold values from 0 to 255, as said below
Outputs:
- dup_score: float32 [196608], P(('corpus', 'group'))
- typical: float32 [196608], P(('corpus', 'group'))
Inputs may be any that keep to these rules, and one draw needn't show every extreme that they name: `labels`: in the rows of one device no cluster is named by more than 6 rows, and some cluster by exactly 6; every cluster is named by some row. `neighbours`: each cluster is the neighbour of exactly one cluster, and never its own.
All inputs are finite; a program needn't handle non-finite values.
Results may differ from a plain program's by a relative error of at most 0.0013.
Values may be sent and summed in bfloat16 or wider, within the bound.
No kernel may reach another device: no remote copies, remote signals or barrier semaphores. Data moves between devices by JAX's collectives and lax.ppermute only.
A program may use at most 128 MiB of HBM per device.

v0:
```python
import math
import jax
import jax.numpy as jnp
from jax import lax
from jax.sharding import PartitionSpec as P

MOST = 6
SHARPNESS = 16.0
TYPICAL_SCALE = 8.0
EPSILON = 1e-06


def normalize(values):
    return values * lax.rsqrt(jnp.sum(values * values, axis=-1, keepdims=True) + EPSILON)


def lookup(lookup_table, positions):
    table_ids = jnp.arange(lookup_table.shape[0], dtype=jnp.int32)
    matches = positions[:, None] == table_ids[None, :]
    return jnp.sum(
        jnp.where(matches, lookup_table[None, :], jnp.zeros_like(lookup_table)[None, :]), axis=1
    )


def fill_slots(unit_embed, positions, slot_total):
    row_ids = jnp.arange(unit_embed.shape[0], dtype=jnp.int32)
    source = jnp.full((slot_total,), -1, jnp.int32).at[positions].set(row_ids)
    present = source >= 0
    picked = jnp.take(unit_embed, jnp.maximum(source, 0), axis=0)
    picked = jnp.where(present[:, None], picked, jnp.zeros_like(picked))
    return (picked, present.astype(jnp.bfloat16))


def pair_sums(block_rows, col_rows, col_mask, distinct):
    similarity = lax.dot_general(
        block_rows, col_rows, (((1,), (1,)), ((), ())), preferred_element_type=jnp.float32
    )
    weights = jnp.exp(SHARPNESS * similarity) * col_mask.astype(jnp.float32)[None, :]
    if distinct is not None:
        weights = jnp.where(distinct, weights, 0.0)
    return jnp.sum(weights, axis=1)


def body(embeddings, labels, neighbours):
    corpus_size = lax.axis_size("corpus")
    group_size = lax.axis_size("group")
    row_count, feature_width = embeddings.shape
    clusters = neighbours.shape[0]
    per_owner = clusters // corpus_size
    per_device = clusters // (corpus_size * group_size)
    slot_total = clusters * MOST
    unit_embed = normalize(embeddings).astype(jnp.bfloat16)
    row_label = labels[:, 0]
    cluster_ids = jnp.arange(clusters, dtype=jnp.int32)
    previous = jnp.sum(
        jnp.where(neighbours[None, :] == cluster_ids[:, None], cluster_ids[None, :], 0), axis=1
    )
    row_ids = jnp.arange(row_count, dtype=jnp.int32)
    before = (row_label[None, :] == row_label[:, None]) & (row_ids[None, :] < row_ids[:, None])
    row_slot = jnp.sum(before.astype(jnp.int32), axis=1)
    near_label = lookup(previous, row_label)
    own_owner = row_label // per_owner
    own_rank = row_label % per_owner
    near_owner = near_label // per_owner
    near_rank = near_label % per_owner
    corpus_at = lax.axis_index("corpus")
    group_at = lax.axis_index("group")
    member_hot = (row_label[:, None] == cluster_ids[None, :]).astype(jnp.bfloat16)
    cluster_sums = lax.dot_general(
        member_hot, unit_embed, (((0,), (0,)), ((), ())), preferred_element_type=jnp.float32
    )
    local_counts = jnp.sum(member_hot, axis=0, dtype=jnp.float32)
    cluster_sums, counts = lax.psum((cluster_sums, local_counts), ("corpus", "group"))
    centroid = normalize(cluster_sums)
    typical_rows = TYPICAL_SCALE * jnp.sum(
        unit_embed * jnp.take(centroid, row_label, axis=0), axis=1
    )

    def slot_of(owner_at, rank_at):
        return (
            (owner_at * group_size + rank_at % group_size) * per_device + rank_at // group_size
        ) * MOST + row_slot

    member_buf, member_mask = fill_slots(unit_embed, slot_of(own_owner, own_rank), slot_total)
    near_buf, near_mask = fill_slots(unit_embed, slot_of(near_owner, near_rank), slot_total)
    shape_rows = (corpus_size, group_size, per_device, MOST, feature_width)
    shape_mask = (corpus_size, group_size, per_device, MOST)
    arrived = (
        lax.all_to_all(
            lax.all_to_all(
                member_buf.reshape(shape_rows), "corpus", split_axis=0, concat_axis=3, tiled=True
            ),
            "group",
            split_axis=1,
            concat_axis=3,
            tiled=True,
        ),
        lax.all_to_all(
            lax.all_to_all(
                near_buf.reshape(shape_rows), "corpus", split_axis=0, concat_axis=3, tiled=True
            ),
            "group",
            split_axis=1,
            concat_axis=3,
            tiled=True,
        ),
        lax.all_to_all(
            lax.all_to_all(
                member_mask.reshape(shape_mask), "corpus", split_axis=0, concat_axis=3, tiled=True
            ),
            "group",
            split_axis=1,
            concat_axis=3,
            tiled=True,
        ),
        lax.all_to_all(
            lax.all_to_all(
                near_mask.reshape(shape_mask), "corpus", split_axis=0, concat_axis=3, tiled=True
            ),
            "group",
            split_axis=1,
            concat_axis=3,
            tiled=True,
        ),
    )
    cluster_span = group_size * corpus_size * MOST
    member_rows = arrived[0].reshape(per_device, cluster_span, feature_width)
    other_rows = arrived[1].reshape(per_device, cluster_span, feature_width)
    member_valid = arrived[2].reshape(per_device, cluster_span)
    other_valid = arrived[3].reshape(per_device, cluster_span)
    mine = corpus_at * per_owner + jnp.arange(per_device, dtype=jnp.int32) * group_size + group_at
    own_count = lookup(counts, mine)
    near_count = lookup(counts, lookup(neighbours, mine))
    block_size = math.gcd(cluster_span, 1024)
    col_ids = jnp.arange(cluster_span, dtype=jnp.int32)

    def one_cluster(cluster_item):
        members, others, member_flags, other_flags, count_own, count_near = cluster_item

        def one_block(first_row):
            block_rows = lax.dynamic_slice_in_dim(members, first_row, block_size, 0)
            distinct = (first_row + jnp.arange(block_size, dtype=jnp.int32))[:, None] != col_ids[
                None, :
            ]
            return (
                pair_sums(block_rows, members, member_flags, distinct),
                pair_sums(block_rows, others, other_flags, None),
            )

        own_sum, near_sum = lax.map(
            one_block, jnp.arange(cluster_span // block_size, dtype=jnp.int32) * block_size
        )
        return jnp.log(
            1.0
            + own_sum.reshape(cluster_span) / count_own
            + near_sum.reshape(cluster_span) / count_near
        )

    scores = lax.map(
        one_cluster, (member_rows, other_rows, member_valid, other_valid, own_count, near_count)
    )
    payload = scores[None]
    layers = payload.shape[0]
    payload = payload.reshape(layers, 1, per_device, group_size, corpus_size, MOST)
    returned = lax.all_to_all(
        lax.all_to_all(payload, "corpus", split_axis=4, concat_axis=1, tiled=True),
        "group",
        split_axis=3,
        concat_axis=4,
        tiled=True,
    )
    returned = returned.reshape(layers, slot_total)
    home_slot = (
        (own_owner * per_device + own_rank // group_size) * group_size + own_rank % group_size
    ) * MOST + row_slot
    dup_score = jnp.take(returned[0], home_slot)
    return (dup_score, typical_rows)


def solution(mesh):
    placed = (P(("corpus", "group"), None), P(("corpus", "group"), None), P())
    return jax.shard_map(
        body,
        mesh=mesh,
        in_specs=placed,
        out_specs=(P(("corpus", "group")), P(("corpus", "group"))),
        check_vma=False,
    )
```

profile of v0, /device:TPU:1, one launch (start us, length us, event | category | flops | bytes accessed | tf_op | source)
XLA Modules:
  0.0 593.5 jit_solution(3198293003437910147)
XLA Ops:
  10.1 1.9 fusion.28
  12.7 3.4 scatter_custom_fusion.1
  17.5 12.0 %all-to-all-start.6 = ((bf16[32,8,1,6]{3,1,2,0:T(8,128)(2,1)}), bf16[32,8,1,6]{3,1,2,0:T(8,128)(2,1)}, u32[]{:S(2)}, u32[]{:S(2)}) async-start(bf16[32,8,1,6]{3,1,2,0:T(8,128)(2,1)} %bitcast.11), calls=%async_computation.6 | async-start | bytes 131072 | tf_op jit(solution)/shard_map/all_to_all | solution.py:117
  29.5 1.9 multiply_reduce_fusion.1
  32.2 3.5 scatter_custom_fusion
  36.3 1.5 reshape.324
  38.3 8.8 %all-to-all-start.2 = ((bf16[32,8,1,6]{3,1,2,0:T(8,128)(2,1)}), bf16[32,8,1,6]{3,1,2,0:T(8,128)(2,1)}, u32[]{:S(2)}, u32[]{:S(2)}) async-start(bf16[32,8,1,6]{3,1,2,0:T(8,128)(2,1)} %bitcast.58), calls=%async_computation.2 | async-start | bytes 131072 | tf_op jit(solution)/shard_map/all_to_all | solution.py:108
  48.3 1.6 copy.45
  51.4 1.6 all_to_all.126
  52.9 2.9 all-to-all-done.2
  55.9 7.1 %all-to-all-start.7 = ((bf16[1,8,1,192]{3,2,0,1:T(2,128)(2,1)}), bf16[1,8,1,192]{3,2,0,1:T(2,128)(2,1)}, u32[]{:S(2)}, u32[]{:S(2)}) async-start(bf16[1,8,1,192]{3,2,0,1:T(2,128)(2,1)} %all_to_all.126), calls=%async_computation.7 | async-start | bytes 16384 | tf_op jit(solution)/shard_map/all_to_all | solution.py:116
  64.3 5.7 gather_fusion.3
  70.0 1.6 copy.39
  73.1 1.6 all_to_all.125
  74.6 4.8 all-to-all-start.3
  79.4 3.4 select_select_fusion
  82.8 5.0 reshape.320
  87.8 3.9 copy.42
  91.7 5.5 all-to-all-start.4
  97.2 5.7 gather_fusion.2
  103.0 3.4 select_select_fusion.1
  106.3 5.0 reshape.317
  111.4 3.9 copy.36
  115.3 35.8 %all-to-all-done.4 = bf16[32,8,1,6,768]{4,1,3,2,0:T(8,128)(2,1)} async-done(((bf16[32,8,1,6,768]{4,1,3,2,0:T(8,128)(2,1)}), bf16[32,8,1,6,768]{4,1,3,2,0:T(8,128)(2,1)}, u32[]{:S(2)}, u32[]{:S(2)}) %all-to-all-start.4) | async-done | bytes 2359328 | tf_op jit(solution)/shard_map/all_to_all | solution.py:99
  151.2 7.6 %all-to-all-start = ((bf16[32,8,1,6,768]{4,1,3,2,0:T(8,128)(2,1)}), bf16[32,8,1,6,768]{4,1,3,2,0:T(8,128)(2,1)}, u32[]{:S(2)}, u32[]{:S(2)}) async-start(bf16[32,8,1,6,768]{4,1,3,2,0:T(8,128)(2,1)} %copy.36), calls=%async_computation | async-start | bytes 4718592 | tf_op jit(solution)/shard_map/all_to_all | solution.py:90
  158.7 3.5 copy.43
  162.2 50.3 %all-to-all-done = bf16[32,8,1,6,768]{4,1,3,2,0:T(8,128)(2,1)} async-done(((bf16[32,8,1,6,768]{4,1,3,2,0:T(8,128)(2,1)}), bf16[32,8,1,6,768]{4,1,3,2,0:T(8,128)(2,1)}, u32[]{:S(2)}, u32[]{:S(2)}) %all-to-all-start) | async-done | bytes 2359328 | tf_op jit(solution)/shard_map/all_to_all | solution.py:90
  212.5 7.1 %all-to-all-start.5 = ((bf16[1,8,1,192,768]{4,3,2,0,1:T(8,128)(2,1)}), bf16[1,8,1,192,768]{4,3,2,0,1:T(8,128)(2,1)}, u32[]{:S(2)}, u32[]{:S(2)}) async-start(bf16[1,8,1,192,768]{4,3,2,0,1:T(8,128)(2,1)} %copy.43), calls=%async_computation.5 | async-start | bytes 4718592 | tf_op jit(solution)/shard_map/all_to_all | solution.py:98
  219.6 3.5 copy.37
  223.1 25.8 %all-to-all-done.5 = bf16[1,8,1,192,768]{4,3,2,0,1:T(8,128)(2,1)} async-done(((bf16[1,8,1,192,768]{4,3,2,0,1:T(8,128)(2,1)}), bf16[1,8,1,192,768]{4,3,2,0,1:T(8,128)(2,1)}, u32[]{:S(2)}, u32[]{:S(2)}) %all-to-all-start.5) | async-done | bytes 2359328 | tf_op jit(solution)/shard_map/all_to_all | solution.py:98
  248.9 5.1 all-to-all-start.1
  254.0 1.6 fusion.14
  258.5 91.5 %psum.14 = f32[256]{0:T(256)S(1)} all-reduce(f32[256]{0:T(256)S(1)} %convert_reduce_fusion.1), channel_id=1, replica_groups=mesh['corpus'=32,'group'=8] {'corpus','group'}, use_global_device_ids=true, to_apply=%region_11.13 | all-reduce | flops 256 | bytes 2048 | tf_op jit(solution)/shard_map/psum | solution.py:73
  353.7 161.5 %all-reduce.2.cloned.1.call-done = f32[256,768]{1,0:T(8,128)} async-done(((f32[256,768]{1,0:T(8,128)}), f32[256,768]{1,0:T(8,128)}) %all-reduce.2.cloned.1.call-update) | async-done | bytes 786448 | tf_op jit(solution)/shard_map/psum | solution.py:73
  516.5 31.4 %while.21 = (s32[]{:T(128)}, f32[3,512]{1,0:T(4,128)S(1)}, f32[3,512]{1,0:T(4,128)S(1)}, s32[3]{0:T(128)S(1)}, bf16[1536,768]{1,0:T(8,128)(2,1)}, /*index=5*/bf1...) while((s32[]{:T(128)}, f32[3,512]{1,0:T(4,128)S(1)}, ...), condition=%wide.region_9.11_spmd.clone, body=%wide.region_6.10_spmd.clone.sunk | while | flops 2422213120 | bytes 6338743 | solution.py:150
  519.7 3.5 fusion.45
  523.2 3.6 fusion.44
  530.1 3.5 fusion.45
  533.7 3.6 fusion.44
  540.6 3.5 fusion.45
  544.2 3.6 fusion.44
  550.1 9.5 %all-to-all-start.8 = ((f32[1,1,1,8,32,6]{3,2,5,1,0,4:T(1,128)}), f32[1,1,1,8,32,6]{3,2,5,1,0,4:T(1,128)S(1)}, u32[]{:S(2)}, u32[]{:S(2)}) async-start(f32[1,1,1,8,32,6]{3,2,5,1,0,4:T(1,128)} %copy.48), calls=%async_computation.8 | async-start | bytes 196608 | tf_op jit(solution)/shard_map/all_to_all | solution.py:166
  560.8 3.5 gather_fusion.1
  564.3 4.4 all-to-all-done.8
  570.7 5.3 all-to-all-start.9
  576.0 2.2 multiply_reduce_fusion
  578.2 2.4 all-to-all-done.9
  581.6 4.5 gather_fusion
  (77 shorter events, 31.3 us)
Async XLA Ops:
  7.2 24.2 %copy-start = (f32[768,768]{1,0:T(8,128)S(1)}, f32[768,768]{1,0:T(8,128)}, u32[]{:S(2)}) copy-start(f32[768,768]{1,0:T(8,128)} %param.7) | copy-start | bytes 7077892
  16.1 15.3 %copy-start.1 = (s32[1536]{0:T(1024)}, s32[1536]{0:T(1024)S(1)}, u32[]{:S(2)}) copy-start(s32[1536]{0:T(1024)S(1)} %scatter_custom_fusion.1) | copy-start | bytes 18436
  17.5 20.8 %all-to-all-start.6 = ((bf16[32,8,1,6]{3,1,2,0:T(8,128)(2,1)}), bf16[32,8,1,6]{3,1,2,0:T(8,128)(2,1)}, u32[]{:S(2)}, u32[]{:S(2)}) async-start(bf16[32,8,1,6]{3,1,2,0:T(8,128)(2,1)} %bitcast.11), calls=%async_computation.6 | async-start | bytes 131072 | tf_op jit(solution)/shard_map/all_to_all | solution.py:117
  38.3 17.6 %all-to-all-start.2 = ((bf16[32,8,1,6]{3,1,2,0:T(8,128)(2,1)}), bf16[32,8,1,6]{3,1,2,0:T(8,128)(2,1)}, u32[]{:S(2)}, u32[]{:S(2)}) async-start(bf16[32,8,1,6]{3,1,2,0:T(8,128)(2,1)} %bitcast.58), calls=%async_computation.2 | async-start | bytes 131072 | tf_op jit(solution)/shard_map/all_to_all | solution.py:108
  55.9 18.8 %all-to-all-start.7 = ((bf16[1,8,1,192]{3,2,0,1:T(2,128)(2,1)}), bf16[1,8,1,192]{3,2,0,1:T(2,128)(2,1)}, u32[]{:S(2)}, u32[]{:S(2)}) async-start(bf16[1,8,1,192]{3,2,0,1:T(2,128)(2,1)} %all_to_all.126), calls=%async_computation.7 | async-start | bytes 16384 | tf_op jit(solution)/shard_map/all_to_all | solution.py:116
  74.6 17.1 %all-to-all-start.3 = ((bf16[1,8,1,192]{3,2,0,1:T(2,128)(2,1)}), bf16[1,8,1,192]{3,2,0,1:T(2,128)(2,1)}, u32[]{:S(2)}, u32[]{:S(2)}) async-start(bf16[1,8,1,192]{3,2,0,1:T(2,128)(2,1)} %all_to_all.125), calls=%async_computation.3 | async-start | bytes 16384 | tf_op jit(solution)/shard_map/all_to_all | solution.py:107
  91.7 59.4 %all-to-all-start.4 = ((bf16[32,8,1,6,768]{4,1,3,2,0:T(8,128)(2,1)}), bf16[32,8,1,6,768]{4,1,3,2,0:T(8,128)(2,1)}, u32[]{:S(2)}, u32[]{:S(2)}) async-start(bf16[32,8,1,6,768]{4,1,3,2,0:T(8,128)(2,1)} %copy.42), calls=%async_computation.4 | async-start | bytes 4718592 | tf_op jit(solution)/shard_map/all_to_all | solution.py:99
  151.2 61.4 %all-to-all-start = ((bf16[32,8,1,6,768]{4,1,3,2,0:T(8,128)(2,1)}), bf16[32,8,1,6,768]{4,1,3,2,0:T(8,128)(2,1)}, u32[]{:S(2)}, u32[]{:S(2)}) async-start(bf16[32,8,1,6,768]{4,1,3,2,0:T(8,128)(2,1)} %copy.36), calls=%async_computation | async-start | bytes 4718592 | tf_op jit(solution)/shard_map/all_to_all | solution.py:90
  212.5 36.4 %all-to-all-start.5 = ((bf16[1,8,1,192,768]{4,3,2,0,1:T(8,128)(2,1)}), bf16[1,8,1,192,768]{4,3,2,0,1:T(8,128)(2,1)}, u32[]{:S(2)}, u32[]{:S(2)}) async-start(bf16[1,8,1,192,768]{4,3,2,0,1:T(8,128)(2,1)} %copy.43), calls=%async_computation.5 | async-start | bytes 4718592 | tf_op jit(solution)/shard_map/all_to_all | solution.py:98
  248.9 267.6 %all-to-all-start.1 = ((bf16[1,8,1,192,768]{4,3,2,0,1:T(8,128)(2,1)}), bf16[1,8,1,192,768]{4,3,2,0,1:T(8,128)(2,1)}, u32[]{:S(2)}, u32[]{:S(2)}) async-start(bf16[1,8,1,192,768]{4,3,2,0,1:T(8,128)(2,1)} %copy.37), calls=%async_computation.1 | async-start | bytes 4718592 | tf_op jit(solution)/shard_map/all_to_all | solution.py:89
  254.0 98.0 %copy-start.2 = (s32[768,1]{0,1:T(1,128)S(1)}, s32[768,1]{0,1:T(1,128)}, u32[]{:S(2)}) copy-start(s32[768,1]{0,1:T(1,128)} %param.8) | copy-start | bytes 9220
  254.0 261.2 %all-reduce.2.cloned.1.call-start = ((), (), s32[]{:S(2)}) async-start(), calls=%async_computation.10 | async-start | bytes 1572864 | tf_op jit(solution)/shard_map/psum | solution.py:73
  550.1 18.6 %all-to-all-start.8 = ((f32[1,1,1,8,32,6]{3,2,5,1,0,4:T(1,128)}), f32[1,1,1,8,32,6]{3,2,5,1,0,4:T(1,128)S(1)}, u32[]{:S(2)}, u32[]{:S(2)}) async-start(f32[1,1,1,8,32,6]{3,2,5,1,0,4:T(1,128)} %copy.48), calls=%async_computation.8 | async-start | bytes 196608 | tf_op jit(solution)/shard_map/all_to_all | solution.py:166
  570.7 9.9 %all-to-all-start.9 = ((f32[8,1,192]{2,1,0:T(1,128)}), f32[8,1,192]{2,1,0:T(1,128)S(1)}, u32[]{:S(2)}, u32[]{:S(2)}) async-start(f32[8,1,192]{2,1,0:T(1,128)} %reshape.394), calls=%async_computation.9 | async-start | bytes 16384 | tf_op jit(solution)/shard_map/all_to_all | solution.py:165
Sparse Core Ops, SparseCore 0:
  260.3 254.8 all-reduce.1
where the time goes:
time: 596 us; the launch traced here: 594 us
  waiting for transfers between devices  284 us (48%)
  blocking collectives  91.5 us (15%)
  starting transfers between devices  72.7 us (12%)
  local copies, waits for them, and re-layouts  68.2 us (11%)
  other arithmetic  34.3 us (6%)
  matrix products  23 us (4%)
  between operations  14.3 us (2%)
  loops' own time  5.96 us (1%)
    psum x1, waiting for transfers between devices, body(): lax.psum((cluster_sums, local_counts), ('corpus', 'group'))  161 us
    psum x1, blocking collectives, body(): lax.psum((cluster_sums, local_counts), ('corpus', 'group'))  91.5 us
    all_to_all x1, waiting for transfers between devices, body(): lax.all_to_all(member_buf.reshape(shape_rows), 'corpus', split_axis=0, co...  50.3 us
    all_to_all x1, waiting for transfers between devices, body(): lax.all_to_all(near_buf.reshape(shape_rows), 'corpus', split_axis=0, conc...  35.8 us
    all_to_all x1, waiting for transfers between devices, body(): lax.all_to_all(lax.all_to_all(near_buf.reshape(shape_rows), 'corpus', spl...  25.8 us
    dot_general x6, matrix products, pair_sums(): lax.dot_general(block_rows, col_rows, (((1,), (1,)), ((), ())), preferred...  21.4 us
    all_to_all x1, starting transfers between devices, body(): lax.all_to_all(near_mask.reshape(shape_mask), 'corpus', split_axis=0, con...  12 us
  transfers between devices with their start and end apart: 11, of which 8 were waited for; matrix products, arithmetic and copies ran while one was open for 13% of the time, Pallas kernels for 0%

commit v1 on v0

--- a/solution.py
+++ b/solution.py
@@ -70,7 +70,7 @@
         member_hot, unit_embed, (((0,), (0,)), ((), ())), preferred_element_type=jnp.float32
     )
     local_counts = jnp.sum(member_hot, axis=0, dtype=jnp.float32)
-    cluster_sums, counts = lax.psum((cluster_sums, local_counts), ("corpus", "group"))
+    cluster_sums, counts = lax.psum(lax.psum((cluster_sums, local_counts), "corpus"), "group")
     centroid = normalize(cluster_sums)
     typical_rows = TYPICAL_SCALE * jnp.sum(
         unit_embed * jnp.take(centroid, row_label, axis=0), axis=1

time: 596 us -> 568 us (0.953)
  waiting for transfers between devices: 284 us -> 263 us
    psum x1 -> x2, waiting for transfers between devices: 161 us -> 141 us  [the longest x1 141 us: body(): lax.psum((cluster_sums, local_counts), 'corpus')]
    psum x1 -> x2, blocking collectives: 91.5 us -> 89.5 us  [the longest x1 59.4 us: body(): lax.psum((cluster_sums, local_counts), 'corpus')]
  transfers between devices with their start and end apart: 11 -> 12, of which waited for: 8 -> 8; matrix products, arithmetic and copies ran while one was open for 13% -> 13% of each run, Pallas kernels for 0% -> 0%
where the time goes in v1:
time: 568 us; the launch traced here: 566 us
  waiting for transfers between devices  263 us (46%)
  blocking collectives  89.5 us (16%)
  local copies, waits for them, and re-layouts  68.2 us (12%)
  starting transfers between devices  67.8 us (12%)
  other arithmetic  34.3 us (6%)
  matrix products  22.9 us (4%)
  between operations  14.3 us (3%)
  loops' own time  5.96 us (1%)
    psum x1, waiting for transfers between devices, body(): lax.psum((cluster_sums, local_counts), 'corpus')  141 us
    psum x1, blocking collectives, body(): lax.psum((cluster_sums, local_counts), 'corpus')  59.4 us
    all_to_all x1, waiting for transfers between devices, body(): lax.all_to_all(member_buf.reshape(shape_rows), 'corpus', split_axis=0, co...  50.3 us
    all_to_all x1, waiting for transfers between devices, body(): lax.all_to_all(near_buf.reshape(shape_rows), 'corpus', split_axis=0, conc...  35.8 us
    psum x1, blocking collectives, body(): lax.psum(lax.psum((cluster_sums, local_counts), 'corpus'), 'group')  30 us
    all_to_all x1, waiting for transfers between devices, body(): lax.all_to_all(lax.all_to_all(near_buf.reshape(shape_rows), 'corpus', spl...  25.8 us
    dot_general x6, matrix products, pair_sums(): lax.dot_general(block_rows, col_rows, (((1,), (1,)), ((), ())), preferred...  21.4 us
    all_to_all x1, starting transfers between devices, body(): lax.all_to_all(near_mask.reshape(shape_mask), 'corpus', split_axis=0, con...  12 us
  transfers between devices with their start and end apart: 12, of which 8 were waited for; matrix products, arithmetic and copies ran while one was open for 13% of the time, Pallas kernels for 0%

profile of v1, /device:TPU:1, one launch (start us, length us, event | category | flops | bytes accessed | tf_op | source)
XLA Modules:
  0.0 565.9 jit_solution(15363117828954433257)
XLA Ops:
  10.1 1.9 fusion.28
  12.7 3.4 scatter_custom_fusion.1
  17.5 12.0 %all-to-all-start.6 = ((bf16[32,8,1,6]{3,1,2,0:T(8,128)(2,1)}), bf16[32,8,1,6]{3,1,2,0:T(8,128)(2,1)}, u32[]{:S(2)}, u32[]{:S(2)}) async-start(bf16[32,8,1,6]{3,1,2,0:T(8,128)(2,1)} %bitcast.11), calls=%async_computation.6 | async-start | bytes 131072 | tf_op jit(solution)/shard_map/all_to_all | solution.py:117
  29.5 1.9 multiply_reduce_fusion.1
  32.2 3.5 scatter_custom_fusion
  38.3 8.8 %all-to-all-start.2 = ((bf16[32,8,1,6]{3,1,2,0:T(8,128)(2,1)}), bf16[32,8,1,6]{3,1,2,0:T(8,128)(2,1)}, u32[]{:S(2)}, u32[]{:S(2)}) async-start(bf16[32,8,1,6]{3,1,2,0:T(8,128)(2,1)} %bitcast.58), calls=%async_computation.2 | async-start | bytes 131072 | tf_op jit(solution)/shard_map/all_to_all | solution.py:108
  48.3 1.6 copy.45
  51.4 1.6 all_to_all.126
  52.9 2.9 all-to-all-done.2
  55.9 7.1 %all-to-all-start.7 = ((bf16[1,8,1,192]{3,2,0,1:T(2,128)(2,1)}), bf16[1,8,1,192]{3,2,0,1:T(2,128)(2,1)}, u32[]{:S(2)}, u32[]{:S(2)}) async-start(bf16[1,8,1,192]{3,2,0,1:T(2,128)(2,1)} %all_to_all.126), calls=%async_computation.7 | async-start | bytes 16384 | tf_op jit(solution)/shard_map/all_to_all | solution.py:116
  64.3 5.7 %gather_fusion.3 = bf16[1536,768]{1,0:T(8,128)(2,1)} fusion(bf16[768,768]{1,0:T(8,128)(2,1)S(1)} %multiply_convert_fusion, s32[2048]{0:T(1024)} %pad_clamp_fusion), kind=kCustom, calls=%fused_computation.1.clone | custom fusion | bytes 4724736 | tf_op jit(solution)/shard_map/jit(_take)/gather | solution.py:29
  70.0 1.6 copy.39
  73.1 1.6 all_to_all.125
  74.6 4.8 all-to-all-start.3
  79.4 3.4 select_select_fusion
  82.8 5.0 reshape.320
  87.8 3.9 copy.42
  91.7 5.5 all-to-all-start.4
  97.2 5.7 %gather_fusion.2 = bf16[1536,768]{1,0:T(8,128)(2,1)} fusion(bf16[768,768]{1,0:T(8,128)(2,1)S(1)} %multiply_convert_fusion, s32[2048]{0:T(1024)S(1)} %pad_clamp_fusion.1), kind=kCustom, calls=%fused_computation.clone | custom fusion | bytes 4724736 | tf_op jit(solution)/shard_map/jit(_take)/gather | solution.py:29
  103.0 3.4 select_select_fusion.1
  106.3 5.0 reshape.317
  111.4 3.9 copy.36
  115.3 35.8 %all-to-all-done.4 = bf16[32,8,1,6,768]{4,1,3,2,0:T(8,128)(2,1)} async-done(((bf16[32,8,1,6,768]{4,1,3,2,0:T(8,128)(2,1)}), bf16[32,8,1,6,768]{4,1,3,2,0:T(8,128)(2,1)}, u32[]{:S(2)}, u32[]{:S(2)}) %all-to-all-start.4) | async-done | bytes 2359328 | tf_op jit(solution)/shard_map/all_to_all | solution.py:99
  151.2 7.6 %all-to-all-start = ((bf16[32,8,1,6,768]{4,1,3,2,0:T(8,128)(2,1)}), bf16[32,8,1,6,768]{4,1,3,2,0:T(8,128)(2,1)}, u32[]{:S(2)}, u32[]{:S(2)}) async-start(bf16[32,8,1,6,768]{4,1,3,2,0:T(8,128)(2,1)} %copy.36), calls=%async_computation | async-start | bytes 4718592 | tf_op jit(solution)/shard_map/all_to_all | solution.py:90
  158.7 3.5 copy.43
  162.2 50.3 %all-to-all-done = bf16[32,8,1,6,768]{4,1,3,2,0:T(8,128)(2,1)} async-done(((bf16[32,8,1,6,768]{4,1,3,2,0:T(8,128)(2,1)}), bf16[32,8,1,6,768]{4,1,3,2,0:T(8,128)(2,1)}, u32[]{:S(2)}, u32[]{:S(2)}) %all-to-all-start) | async-done | bytes 2359328 | tf_op jit(solution)/shard_map/all_to_all | solution.py:90
  212.5 7.1 %all-to-all-start.5 = ((bf16[1,8,1,192,768]{4,3,2,0,1:T(8,128)(2,1)}), bf16[1,8,1,192,768]{4,3,2,0,1:T(8,128)(2,1)}, u32[]{:S(2)}, u32[]{:S(2)}) async-start(bf16[1,8,1,192,768]{4,3,2,0,1:T(8,128)(2,1)} %copy.43), calls=%async_computation.5 | async-start | bytes 4718592 | tf_op jit(solution)/shard_map/all_to_all | solution.py:98
  219.6 3.5 copy.37
  223.1 25.8 %all-to-all-done.5 = bf16[1,8,1,192,768]{4,3,2,0,1:T(8,128)(2,1)} async-done(((bf16[1,8,1,192,768]{4,3,2,0,1:T(8,128)(2,1)}), bf16[1,8,1,192,768]{4,3,2,0,1:T(8,128)(2,1)}, u32[]{:S(2)}, u32[]{:S(2)}) %all-to-all-start.5) | async-done | bytes 2359328 | tf_op jit(solution)/shard_map/all_to_all | solution.py:98
  248.9 5.1 all-to-all-start.1
  254.0 1.5 fusion.14
  258.5 140.9 %all-reduce.3.cloned.1.call-done = f32[256,768]{1,0:T(8,128)} async-done(((f32[256,768]{1,0:T(8,128)}), f32[256,768]{1,0:T(8,128)}) %all-reduce.3.cloned.1.call-update) | async-done | bytes 786448 | tf_op jit(solution)/shard_map/psum | solution.py:73
  399.4 59.4 %psum.28 = f32[256]{0:T(256)S(1)} all-reduce(f32[256]{0:T(256)S(1)} %convert_reduce_fusion.1), channel_id=1, replica_groups=mesh['corpus'=32,'group'=8] {'corpus'}, use_global_device_ids=true, to_apply=%region_11.13 | all-reduce | flops 256 | bytes 2048 | tf_op jit(solution)/shard_map/psum | solution.py:73
  458.8 30.0 %psum.29 = f32[256]{0:T(256)S(1)} all-reduce(f32[256]{0:T(256)S(1)} %psum.28), channel_id=1, replica_groups=mesh['corpus'=32,'group'=8] {'group'}, use_global_device_ids=true, to_apply=%region_12.14 | all-reduce | flops 256 | bytes 2048 | tf_op jit(solution)/shard_map/psum | solution.py:73
  493.8 31.4 %while.21 = (s32[]{:T(128)}, f32[3,512]{1,0:T(4,128)S(1)}, f32[3,512]{1,0:T(4,128)S(1)}, s32[3]{0:T(128)S(1)}, bf16[1536,768]{1,0:T(8,128)(2,1)}, /*index=5*/bf1...) while((s32[]{:T(128)}, f32[3,512]{1,0:T(4,128)S(1)}, ...), condition=%wide.region_9.11_spmd.clone, body=%wide.region_6.10_spmd.clone.sunk | while | flops 2422213120 | bytes 6338743 | solution.py:150
  497.0 3.5 fusion.45
  500.6 3.6 fusion.44
  507.5 3.5 fusion.45
  511.0 3.6 fusion.44
  517.9 3.5 fusion.45
  521.5 3.6 fusion.44
  527.4 4.6 all-to-all-start.8
  533.3 3.5 gather_fusion.1
  536.7 4.4 all-to-all-done.8
  543.1 5.2 all-to-all-start.9
  548.3 2.2 multiply_reduce_fusion
  550.5 2.5 all-to-all-done.9
  554.0 4.5 gather_fusion
  (81 shorter events, 32.8 us)
Async XLA Ops:
  7.2 24.2 %copy-start = (f32[768,768]{1,0:T(8,128)S(1)}, f32[768,768]{1,0:T(8,128)}, u32[]{:S(2)}) copy-start(f32[768,768]{1,0:T(8,128)} %param.7) | copy-start | bytes 7077892
  16.1 15.3 %copy-start.1 = (s32[1536]{0:T(1024)}, s32[1536]{0:T(1024)S(1)}, u32[]{:S(2)}) copy-start(s32[1536]{0:T(1024)S(1)} %scatter_custom_fusion.1) | copy-start | bytes 18436
  17.5 20.8 %all-to-all-start.6 = ((bf16[32,8,1,6]{3,1,2,0:T(8,128)(2,1)}), bf16[32,8,1,6]{3,1,2,0:T(8,128)(2,1)}, u32[]{:S(2)}, u32[]{:S(2)}) async-start(bf16[32,8,1,6]{3,1,2,0:T(8,128)(2,1)} %bitcast.11), calls=%async_computation.6 | async-start | bytes 131072 | tf_op jit(solution)/shard_map/all_to_all | solution.py:117
  38.3 17.6 %all-to-all-start.2 = ((bf16[32,8,1,6]{3,1,2,0:T(8,128)(2,1)}), bf16[32,8,1,6]{3,1,2,0:T(8,128)(2,1)}, u32[]{:S(2)}, u32[]{:S(2)}) async-start(bf16[32,8,1,6]{3,1,2,0:T(8,128)(2,1)} %bitcast.58), calls=%async_computation.2 | async-start | bytes 131072 | tf_op jit(solution)/shard_map/all_to_all | solution.py:108
  55.9 18.8 %all-to-all-start.7 = ((bf16[1,8,1,192]{3,2,0,1:T(2,128)(2,1)}), bf16[1,8,1,192]{3,2,0,1:T(2,128)(2,1)}, u32[]{:S(2)}, u32[]{:S(2)}) async-start(bf16[1,8,1,192]{3,2,0,1:T(2,128)(2,1)} %all_to_all.126), calls=%async_computation.7 | async-start | bytes 16384 | tf_op jit(solution)/shard_map/all_to_all | solution.py:116
  74.6 17.1 %all-to-all-start.3 = ((bf16[1,8,1,192]{3,2,0,1:T(2,128)(2,1)}), bf16[1,8,1,192]{3,2,0,1:T(2,128)(2,1)}, u32[]{:S(2)}, u32[]{:S(2)}) async-start(bf16[1,8,1,192]{3,2,0,1:T(2,128)(2,1)} %all_to_all.125), calls=%async_computation.3 | async-start | bytes 16384 | tf_op jit(solution)/shard_map/all_to_all | solution.py:107
  91.7 59.4 %all-to-all-start.4 = ((bf16[32,8,1,6,768]{4,1,3,2,0:T(8,128)(2,1)}), bf16[32,8,1,6,768]{4,1,3,2,0:T(8,128)(2,1)}, u32[]{:S(2)}, u32[]{:S(2)}) async-start(bf16[32,8,1,6,768]{4,1,3,2,0:T(8,128)(2,1)} %copy.42), calls=%async_computation.4 | async-start | bytes 4718592 | tf_op jit(solution)/shard_map/all_to_all | solution.py:99
  151.2 61.4 %all-to-all-start = ((bf16[32,8,1,6,768]{4,1,3,2,0:T(8,128)(2,1)}), bf16[32,8,1,6,768]{4,1,3,2,0:T(8,128)(2,1)}, u32[]{:S(2)}, u32[]{:S(2)}) async-start(bf16[32,8,1,6,768]{4,1,3,2,0:T(8,128)(2,1)} %copy.36), calls=%async_computation | async-start | bytes 4718592 | tf_op jit(solution)/shard_map/all_to_all | solution.py:90
  212.5 36.4 %all-to-all-start.5 = ((bf16[1,8,1,192,768]{4,3,2,0,1:T(8,128)(2,1)}), bf16[1,8,1,192,768]{4,3,2,0,1:T(8,128)(2,1)}, u32[]{:S(2)}, u32[]{:S(2)}) async-start(bf16[1,8,1,192,768]{4,3,2,0,1:T(8,128)(2,1)} %copy.43), calls=%async_computation.5 | async-start | bytes 4718592 | tf_op jit(solution)/shard_map/all_to_all | solution.py:98
  248.9 244.9 %all-to-all-start.1 = ((bf16[1,8,1,192,768]{4,3,2,0,1:T(8,128)(2,1)}), bf16[1,8,1,192,768]{4,3,2,0,1:T(8,128)(2,1)}, u32[]{:S(2)}, u32[]{:S(2)}) async-start(bf16[1,8,1,192,768]{4,3,2,0,1:T(8,128)(2,1)} %copy.37), calls=%async_computation.1 | async-start | bytes 4718592 | tf_op jit(solution)/shard_map/all_to_all | solution.py:89
  254.0 236.8 %copy-start.2 = (s32[768,1]{0,1:T(1,128)S(1)}, s32[768,1]{0,1:T(1,128)}, u32[]{:S(2)}) copy-start(s32[768,1]{0,1:T(1,128)} %param.8) | copy-start | bytes 9220
  254.0 145.4 %all-reduce.3.cloned.1.call-start = ((), (), s32[]{:S(2)}) async-start(), calls=%async_computation.10 | async-start | bytes 1572864 | tf_op jit(solution)/shard_map/psum | solution.py:73
  255.6 237.0 %all-reduce.5.cloned.1.call-start = ((), (), s32[]{:S(2)}) async-start(), calls=%async_computation.11 | async-start | bytes 1572864 | tf_op jit(solution)/shard_map/psum | solution.py:73
  527.4 13.7 %all-to-all-start.8 = ((f32[1,1,1,8,32,6]{3,2,5,1,0,4:T(1,128)}), f32[1,1,1,8,32,6]{3,2,5,1,0,4:T(1,128)S(1)}, u32[]{:S(2)}, u32[]{:S(2)}) async-start(f32[1,1,1,8,32,6]{3,2,5,1,0,4:T(1,128)} %copy.48), calls=%async_computation.8 | async-start | bytes 196608 | tf_op jit(solution)/shard_map/all_to_all | solution.py:166
  543.1 9.8 %all-to-all-start.9 = ((f32[8,1,192]{2,1,0:T(1,128)}), f32[8,1,192]{2,1,0:T(1,128)S(1)}, u32[]{:S(2)}, u32[]{:S(2)}) async-start(f32[8,1,192]{2,1,0:T(1,128)} %reshape.394), calls=%async_computation.9 | async-start | bytes 16384 | tf_op jit(solution)/shard_map/all_to_all | solution.py:165
Sparse Core Ops, SparseCore 0:
  258.2 141.1 all-reduce.2
  401.7 66.9 all-reduce.4
